TPU v7x, 256 devices: a whole 4x4x8 slice. The times are simulated.
256 devices in a mesh: expert: 8 (over x, core), tensor: 32 (over z, y).
Axes of the slice: x: 4, y: 4, z: 8, core: 2. Of those that a mesh axis runs over, the one named last changes fastest.
Arguments:
- resid: bfloat16 [16384, 2048], P(('expert', 'tensor')), may hold values from -6 to 6
- contexts: bfloat16 [16384, 4096], P('expert', 'tensor'), may hold values from -6 to 6
- att_routes: int32 [16384, 2], P('expert'), may hold values from 0 to 7, all different within a row
- att_scores: float32 [16384, 2], P('expert'), may hold values from -6 to 6
- att_out_w: bfloat16 [8, 2048, 2048], P(None, 'tensor'), may hold values from -0.125 to 0.125
- norm_gain: bfloat16 [2048], replicated, may hold values from 0.25 to 1.75
- router_w: bfloat16 [2048, 8], replicated, may hold values from -0.125 to 0.125
- mlp_routes: int32 [16384, 2], P(('expert', 'tensor')), may hold values from 0 to 7, all different within a row
- split_rule: int32 [16384, 2], P(('expert', 'tensor')), may hold values from 0 to 2519
- placement: int32 [32], replicated, may hold values from 0 to 7, as said below
- cap_blocks: int32 [32], replicated, may hold values from 1 to 2, as said below
- w_gate_up: bfloat16 [32, 2048, 2, 5632], P('tensor', None, None, 'expert'), as said below
- w_down: bfloat16 [32, 5632, 2048], P('tensor', 'expert'), as said below
- final_gain: bfloat16 [2048], replicated, may hold values from 0.25 to 1.75
Outputs:
- stream_out: bfloat16 [16384, 2048], P(('expert', 'tensor'))
- normalized: bfloat16 [16384, 2048], P(('expert', 'tensor'))
Inputs may be any that keep to these rules, and one draw needn't show every extreme that they name: `att_routes`: each row names 2 different experts. `mlp_routes`: each row names 2 different experts. `placement`: every expert is held by at least one slot. `cap_blocks`: some slot accepts 2 blocks. `w_gate_up`: slots that hold the same expert hold equal weights. `w_down`: slots that hold the same expert hold equal weights.
All inputs are finite; a program needn't handle non-finite values.
Results may differ from a plain program's by a relative error of at most 0.023.
Values may be sent and summed in bfloat16 or wider, within the bound.
No kernel may reach another device: no remote copies, remote signals or barrier semaphores. Data moves between devices by JAX's collectives and lax.ppermute only.
A program may use at most 64 MiB of HBM per device.

v0:
```python
import jax
import jax.numpy as jnp
from jax import lax
from jax.sharding import Mesh, PartitionSpec as P

MAXB = 2
TENSOR = ("tz", "ty")
norm_eps = 1e-06


def rms_norm(values, gain):
    scale = lax.rsqrt(jnp.mean(values * values, axis=-1, keepdims=True) + norm_eps)
    return values * scale * gain.astype(values.dtype)


def pair_gates(scores):
    first = jax.nn.silu(scores[:, 0:1] * 0.0) * 0.0 + jax.nn.sigmoid(
        scores[:, 0:1] - scores[:, 1:2]
    )
    first = first[:, 0]
    return jnp.stack([first, 1.0 - first], axis=1)


def activate(shard_piece, w_gate_up):
    both = jnp.einsum(
        "tsecd,sdgf->tsecgf", shard_piece, w_gate_up, preferred_element_type=jnp.float32
    )
    hidden = (jax.nn.silu(both[:, :, :, :, 0, :]) * both[:, :, :, :, 1, :]).astype(jnp.bfloat16)
    hidden = jnp.transpose(hidden, (0, 2, 3, 1, 4))
    return hidden.reshape(
        hidden.shape[0] * hidden.shape[1] * hidden.shape[2], hidden.shape[3], hidden.shape[4]
    )


def per_device(
    resid,
    contexts,
    att_routes,
    att_scores,
    att_out_w,
    norm_gain,
    router_w,
    mlp_routes,
    split_rule,
    placement,
    cap_blocks,
    w_gate_up,
    w_down,
    final_gain,
):
    n_tensor = lax.axis_size(TENSOR)
    row_count = resid.shape[0]
    model_width = resid.shape[1]
    group_rows = contexts.shape[0]
    att_experts = att_out_w.shape[0]
    slice_ctx = att_out_w.shape[1]
    top_count = att_routes.shape[1]
    gate_att = pair_gates(att_scores)
    chosen = (
        att_routes[:, :, None] == jnp.arange(att_experts, dtype=jnp.int32)[None, None, :]
    ).astype(jnp.float32)
    weighted = chosen * gate_att[:, :, None]
    context_part = contexts.reshape(group_rows, slice_ctx, top_count).astype(jnp.float32)
    mixed = (
        jnp.einsum("tke,tck->tec", weighted, context_part)
        .astype(jnp.bfloat16)
        .reshape(group_rows, att_experts * slice_ctx)
    )
    weight_flat = att_out_w.reshape(att_experts * slice_ctx, model_width)
    row_block = mixed
    partial = jnp.dot(row_block, weight_flat, preferred_element_type=jnp.float32).astype(
        jnp.bfloat16
    )
    partial = lax.psum_scatter(partial, "tz", scatter_dimension=0, tiled=True)
    attention = lax.psum_scatter(partial, "ty", scatter_dimension=0, tiled=True).astype(jnp.float32)
    stream = (resid.astype(jnp.float32) + attention).astype(jnp.bfloat16)
    normed = rms_norm(stream.astype(jnp.float32), norm_gain).astype(jnp.bfloat16)
    logits = jnp.dot(normed, router_w, preferred_element_type=jnp.float32)
    gate_mlp = pair_gates(jnp.take_along_axis(logits, mlp_routes, axis=1))
    replicas = placement.shape[0]
    slots = w_gate_up.shape[0]
    expert_total = router_w.shape[1]
    block_rows = max(1, row_count * top_count // (2 * replicas))
    capacity_rows = MAXB * block_rows
    slot_ids = jnp.arange(replicas, dtype=jnp.int32)
    expert_ids = jnp.arange(expert_total, dtype=jnp.int32)
    copies = jnp.sum((placement[None, :] == expert_ids[:, None]).astype(jnp.int32), axis=1)
    earlier = jnp.sum(
        (
            (placement[None, :] == placement[:, None]) & (slot_ids[None, :] < slot_ids[:, None])
        ).astype(jnp.int32),
        axis=1,
    )
    route_onehot = (mlp_routes[:, :, None] == expert_ids[None, None, :]).astype(jnp.int32)
    route_copies = jnp.sum(route_onehot * copies[None, None, :], axis=2)
    replica_rank = jnp.remainder(split_rule, route_copies)
    match = (
        (placement[None, None, :] == mlp_routes[:, :, None])
        & (earlier[None, None, :] == replica_rank[:, :, None])
    ).astype(jnp.int32)
    replica_slot = jnp.sum(match * slot_ids[None, None, :], axis=2)
    capacity = jnp.sum(match * cap_blocks[None, None, :], axis=2) * block_rows
    flat_match = match.reshape(row_count * top_count, replicas)
    before = jnp.cumsum(flat_match, axis=0) - flat_match
    arrival = jnp.sum(before * flat_match, axis=1).reshape(row_count, top_count)
    is_kept = arrival < capacity
    holder = replica_slot // slots
    within = replica_slot % slots
    position = within * (n_tensor * capacity_rows) + holder * capacity_rows + arrival
    position = jnp.where(is_kept, position, -1)
    buffer_rows = slots * n_tensor * capacity_rows
    placer = jnp.sum(
        (jnp.arange(buffer_rows, dtype=jnp.int32)[:, None, None] == position[None, :, :]).astype(
            jnp.bfloat16
        ),
        axis=2,
    )
    send_rows = jnp.dot(placer, normed, preferred_element_type=jnp.float32).astype(jnp.bfloat16)
    send_rows = send_rows.reshape(slots, n_tensor, capacity_rows, model_width)
    exchanged = lax.all_to_all(send_rows, TENSOR, split_axis=1, concat_axis=1, tiled=True)
    arrived = lax.all_gather(exchanged[None], "expert", axis=0, tiled=True)
    hidden = activate(arrived, w_gate_up)
    row_block = hidden
    summed = lax.psum_scatter(
        jnp.einsum("bsf,sfd->bsd", row_block, w_down, preferred_element_type=jnp.float32).astype(
            jnp.bfloat16
        ),
        "expert",
        scatter_dimension=0,
        tiled=True,
    )
    results = summed.reshape(n_tensor, capacity_rows, slots, model_width)
    returned = lax.all_to_all(results, TENSOR, split_axis=0, concat_axis=0, tiled=True)
    flat_back = returned.reshape(n_tensor * capacity_rows * slots, model_width)
    back_index = jnp.where(is_kept, holder * (capacity_rows * slots) + arrival * slots + within, 0)
    fetched = (
        jnp.take(flat_back, back_index.reshape(-1), axis=0)
        .reshape(row_count, top_count, model_width)
        .astype(jnp.float32)
    )
    factors = gate_mlp * is_kept.astype(jnp.float32)
    expert_mix = fetched[:, 0, :] * factors[:, 0:1] + fetched[:, 1, :] * factors[:, 1:2]
    after = stream.astype(jnp.float32) + expert_mix
    return (after.astype(jnp.bfloat16), rms_norm(after, final_gain).astype(jnp.bfloat16))


def split_mesh(mesh):
    n_expert, n_tensor = mesh.devices.shape
    n_y = 4 if n_tensor % 4 == 0 else 1
    return Mesh(mesh.devices.reshape(n_expert, n_tensor // n_y, n_y), ("expert", "tz", "ty"))


def solution(mesh):
    mesh = split_mesh(mesh)
    return jax.shard_map(
        per_device,
        mesh=mesh,
        in_specs=(
            P(("expert", "tz", "ty"), None),
            P("expert", TENSOR),
            P("expert", None),
            P("expert", None),
            P(None, TENSOR, None),
            P(),
            P(),
            P(("expert", "tz", "ty"), None),
            P(("expert", "tz", "ty"), None),
            P(),
            P(),
            P(TENSOR, None, None, "expert"),
            P(TENSOR, "expert", None),
            P(),
        ),
        out_specs=(P(("expert", "tz", "ty"), None), P(("expert", "tz", "ty"), None)),
        check_vma=False,
    )
```

profile of v0, /device:TPU:7, one launch (start us, length us, event | category | flops | bytes accessed | tf_op | source)
XLA Modules:
  0.0 327.3 jit_solution(1362483452195812732)
XLA Ops:
  7.2 0.0 reduce-scatter.4.cloned.1.call-start
  7.2 2.2 copy.76
  9.4 1.4 reshape.178
  10.8 2.1 copy.77
  12.9 0.1 broadcast_subtract_fusion
  13.0 0.3 copy.75
  13.3 1.4 copy.74
  14.7 14.3 %convolution_convert_fusion = bf16[2048,8,64]{2,1,0:T(8,128)(2,1)S(1)} fusion(bf16[2048,64,2]{1,2,0:T(2,128)(2,1)} %copy.77, bf16[2048,2]{1,0:T(8,128)(2,1)S(1)} %copy.75, s32[2048,2]{1,0:T(8,128)} %copy.74), kind=kOutput, calls=%fused_computation.13 | convolution fusion | flops 4259840 | bytes 2646016 | tf_op jit(solution)/shard_map/tke,tck->tec/dot_general | solution.py:65
  29.0 7.0 %bitcast_convert_fusion = bf16[2048,2048]{1,0:T(8,128)(2,1)} fusion(bf16[8,64,2048]{2,1,0:T(8,128)(2,1)S(1)} %copy-done.11, bf16[2048,8,64]{2,1,0:T(8,128)(2,1)S(1)} %convolution_convert_fusion), kind=kOutput, calls=%fused_computation.2 | convolution fusion | flops 4299161600 | bytes 12582912 | tf_op jit(solution)/shard_map/dot_general | solution.py:71
  36.0 0.0 reduce-scatter.4.cloned.1.call-update
  36.0 0.0 reduce-scatter.6.cloned.1.call-start
  36.1 98.0 %reduce-scatter.4.cloned.1.call-done = bf16[256,2048]{1,0:T(8,128)(2,1)} async-done(((bf16[2048,2048]{1,0:T(8,128)(2,1)}), bf16[256,2048]{1,0:T(8,128)(2,1)}) %reduce-scatter.4.cloned.1.call-update) | async-done | bytes 1048592 | tf_op jit(solution)/shard_map/reduce_scatter | solution.py:74
  134.0 0.0 reduce-scatter.6.cloned.1.call-update
  134.1 0.0 all-gather.3.cloned.1.call-start
  134.1 0.1 copy.79
  134.2 0.1 convert_reduce_fusion.1
  134.4 0.1 select_reduce_fusion.3
  134.5 0.1 and_select_fusion.1
  134.6 0.1 copy.80
  134.7 0.1 eq.133
  134.8 0.1 eq.119
  135.0 0.2 convert_reduce_fusion
  135.1 0.1 fusion.26
  135.3 0.2 reduce_window_sum.11
  135.4 0.2 select_reduce_fusion
  135.6 0.1 reduce_sum.92
  135.8 0.1 copy.81
  135.8 0.1 select_reduce_fusion.2
  136.0 0.1 fusion.27
  136.0 23.9 %reduce-scatter.6.cloned.1.call-done = bf16[64,2048]{1,0:T(8,128)(2,1)} async-done(((bf16[256,2048]{1,0:T(8,128)(2,1)}), bf16[64,2048]{1,0:T(8,128)(2,1)}) %reduce-scatter.6.cloned.1.call-update) | async-done | bytes 262160 | tf_op jit(solution)/shard_map/reduce_scatter | solution.py:75
  160.0 1.1 fusion.15
  161.1 1.1 convolution_convert_fusion.1
  162.3 2.0 reshape.179
  164.3 21.4 %all_to_all.10 = bf16[1,32,4,2048]{3,2,0,1:T(4,128)(2,1)S(1)} all-to-all(bf16[1,32,4,2048]{3,2,0,1:T(4,128)(2,1)} %bitcast.82), channel_id=1, replica_groups=mesh['expert'=8,'tz'=8,'ty'=4] {'tz','ty'}, dimensions={1} | all-to-all | bytes 1048576 | tf_op jit(solution)/shard_map/all_to_all | solution.py:120
  185.7 1.1 copy.84
  186.8 0.0 all-gather.3.cloned.1.call-update
  186.8 0.2 reduce-scatter.8.cloned.1.call-start
  187.0 33.9 %all-gather.3.cloned.1.call-done = bf16[8,32,4,2048]{3,1,2,0:T(8,128)(2,1)} async-done(((bf16[1,32,4,2048]{3,1,2,0:T(8,128)(2,1)}), bf16[8,32,4,2048]{3,1,2,0:T(8,128)(2,1)}) %all-gather.3.cloned.1.call-update) | async-done | bytes 4194320 | tf_op jit(solution)/shard_map/all_gather | solution.py:121
  220.9 10.0 %fusion.6 = f32[8,1,32,4,2,704]{5,2,4,3,0,1:T(8,128)S(1)} fusion(bf16[1,2048,2,704]{1,3,2,0:T(8,128)(2,1)} %param.25, bf16[8,32,4,2048]{3,1,2,0:T(8,128)(2,1)} %all-gather.3.cloned.1.call-done), kind=kOutput, calls=%fused_computation.12 | convolution fusion | flops 5905580032 | bytes 15728640 | tf_op jit(solution)/shard_map/tsecd,sdgf->tsecgf/dot_general | solution.py:25
  230.9 1.0 fusion.4
  231.9 2.4 copy.85
  234.3 3.7 %convert_element_type.95 = bf16[1024,704]{1,0:T(8,128)(2,1)} reshape(bf16[8,1,32,4,1,704]{5,3,2,0,4,1:T(4,128)(2,1)} %copy.85) | data formatting | bytes 2883584 | tf_op jit(solution)/shard_map/convert_element_type | solution.py:28
  238.1 6.4 %convert_bitcast_fusion = bf16[1024,1,2048]{2,0,1:T(8,128)(2,1)} fusion(bf16[1024,704]{1,0:T(8,128)(2,1)} %convert_element_type.95, bf16[1,704,2048]{2,1,0:T(8,128)(2,1)S(1)} %copy-done), kind=kOutput, calls=%fused_computation.7 | convolution fusion | flops 2954887168 | bytes 8519680 | tf_op jit(solution)/shard_map/bsf,sfd->bsd/dot_general | solution.py:125
  244.4 0.0 reduce-scatter.8.cloned.1.call-update
  244.5 0.1 copy.90
  244.6 0.1 reshape.194
  244.7 0.1 copy.88
  244.8 0.1 mul.206
  244.9 0.1 copy.87
  245.0 0.1 mul.205
  245.2 39.8 %reduce-scatter.8.cloned.1.call-done = bf16[128,1,2048]{2,0,1:T(8,128)(2,1)} async-done(((bf16[1024,1,2048]{2,0,1:T(8,128)(2,1)}), bf16[128,1,2048]{2,0,1:T(8,128)(2,1)}) %reduce-scatter.8.cloned.1.call-update) | async-done | bytes 524304 | tf_op jit(solution)/shard_map/reduce_scatter | solution.py:124
  285.0 2.0 reshape.183
  287.1 9.7 %all-to-all-start.1 = ((bf16[32,4,1,2048]{3,1,2,0:T(4,128)(2,1)}), bf16[32,4,1,2048]{3,1,2,0:T(4,128)(2,1)}, u32[]{:S(2)}, u32[]{:S(2)}) async-start(bf16[32,4,1,2048]{3,1,2,0:T(4,128)(2,1)} %bitcast.81), calls=%async_computation.4 | async-start | bytes 1048576 | tf_op jit(solution)/shard_map/all_to_all | solution.py:133
  296.8 0.2 fusion.22
  297.0 1.0 gather_fusion.1
  298.1 0.1 reshape.197
  298.2 0.1 copy.91
  298.3 15.7 %all-to-all-done.1 = bf16[32,4,1,2048]{3,1,2,0:T(4,128)(2,1)} async-done(((bf16[32,4,1,2048]{3,1,2,0:T(4,128)(2,1)}), bf16[32,4,1,2048]{3,1,2,0:T(4,128)(2,1)}, u32[]{:S(2)}, u32[]{:S(2)}) %all-to-all-start.1) | async-done | bytes 524320 | tf_op jit(solution)/shard_map/all_to_all | solution.py:133
  314.1 1.2 reshape.184
  315.2 1.7 gather_fusion
  317.0 1.4 gather.11
  318.3 0.3 fusion.21
  318.7 1.2 multiply_reduce_fusion
  320.0 0.8 multiply_convert_fusion
  (40 shorter events, 0.2 us)
Async XLA Ops:
  7.2 230.9 %copy-start = (bf16[1,704,2048]{2,1,0:T(8,128)(2,1)S(1)}, bf16[1,704,2048]{2,1,0:T(8,128)(2,1)}, u32[]{:S(2)}) copy-start(bf16[1,704,2048]{2,1,0:T(8,128)(2,1)} %param.26) | copy-start | bytes 8650756
  7.2 5.7 %copy-start.5 = (f32[2048,2]{0,1:T(2,128)S(1)}, f32[2048,2]{0,1:T(2,128)}, u32[]{:S(2)}) copy-start(f32[2048,2]{0,1:T(2,128)} %param.17) | copy-start | bytes 49156
  7.2 6.1 %copy-start.4 = (s32[2048,2]{0,1:T(2,128)S(1)}, s32[2048,2]{0,1:T(2,128)}, u32[]{:S(2)}) copy-start(s32[2048,2]{0,1:T(2,128)} %param.16) | copy-start | bytes 49156
  7.2 126.8 %reduce-scatter.4.cloned.1.call-start = ((), (), s32[]{:S(2)}) async-start(), calls=%async_computation.5 | async-start | bytes 9437184 | tf_op jit(solution)/shard_map/reduce_scatter | solution.py:74
  14.7 14.3 %copy-start.11 = (bf16[8,64,2048]{2,1,0:T(8,128)(2,1)S(1)}, bf16[8,64,2048]{2,1,0:T(8,128)(2,1)}, u32[]{:S(2)}) copy-start(bf16[8,64,2048]{2,1,0:T(8,128)(2,1)} %param.18) | copy-start | bytes 6291460
  36.0 98.2 %copy-start.7 = (bf16[2048]{0:T(1024)(128)(2,1)S(1)}, bf16[2048]{0:T(1024)(128)(2,1)}, u32[]{:S(2)}) copy-start(bf16[2048]{0:T(1024)(128)(2,1)} %param.19) | copy-start | bytes 12292
  36.0 98.2 %copy-start.3 = (s32[64,2]{0,1:T(2,128)S(1)}, s32[64,2]{0,1:T(2,128)}, u32[]{:S(2)}) copy-start(s32[64,2]{0,1:T(2,128)} %param.21) | copy-start | bytes 1540
  36.0 98.3 %copy-start.6 = (s32[32]{0:T(128)S(1)}, s32[32]{0:T(128)}, u32[]{:S(2)}) copy-start(s32[32]{0:T(128)} %param.23) | copy-start | bytes 388
  36.0 98.5 %copy-start.9 = (s32[64,2]{0,1:T(2,128)S(1)}, s32[64,2]{0,1:T(2,128)}, u32[]{:S(2)}) copy-start(s32[64,2]{0,1:T(2,128)} %param.22) | copy-start | bytes 1540
  36.0 99.9 %copy-start.10 = (s32[32]{0:T(128)S(1)}, s32[32]{0:T(128)}, u32[]{:S(2)}) copy-start(s32[32]{0:T(128)} %param.24) | copy-start | bytes 388
  36.0 124.0 %copy-start.2 = (bf16[64,2048]{1,0:T(8,128)(2,1)S(1)}, bf16[64,2048]{1,0:T(8,128)(2,1)}, u32[]{:S(2)}) copy-start(bf16[64,2048]{1,0:T(8,128)(2,1)} %param.14) | copy-start | bytes 786436
  36.0 123.9 %reduce-scatter.6.cloned.1.call-start = ((), (), s32[]{:S(2)}) async-start(), calls=%async_computation.6 | async-start | bytes 1310720 | tf_op jit(solution)/shard_map/reduce_scatter | solution.py:75
  134.1 86.9 %all-gather.3.cloned.1.call-start = ((), (), s32[]{:S(2)}) async-start(), calls=%async_computation.8 | async-start | bytes 4718592 | tf_op jit(solution)/shard_map/all_gather | solution.py:121
  161.1 135.7 %copy-start.1 = (bf16[64,2048]{1,0:T(8,128)(2,1)}, bf16[64,2048]{1,0:T(8,128)(2,1)S(1)}, u32[]{:S(2)}) copy-start(bf16[64,2048]{1,0:T(8,128)(2,1)S(1)} %get-tuple-element.9) | copy-start | bytes 786436
  186.8 98.2 %reduce-scatter.8.cloned.1.call-start = ((), (), s32[]{:S(2)}) async-start(), calls=%async_computation.7 | async-start | bytes 4718592 | tf_op jit(solution)/shard_map/reduce_scatter | solution.py:124
  244.4 0.8 copy-start.8
  244.4 52.4 %copy-start.12 = (bf16[2048,8]{0,1:T(8,128)(2,1)S(1)}, bf16[2048,8]{0,1:T(8,128)(2,1)}, u32[]{:S(2)}) copy-start(bf16[2048,8]{0,1:T(8,128)(2,1)} %param.20) | copy-start | bytes 98308
  287.1 27.0 %all-to-all-start.1 = ((bf16[32,4,1,2048]{3,1,2,0:T(4,128)(2,1)}), bf16[32,4,1,2048]{3,1,2,0:T(4,128)(2,1)}, u32[]{:S(2)}, u32[]{:S(2)}) async-start(bf16[32,4,1,2048]{3,1,2,0:T(4,128)(2,1)} %bitcast.81), calls=%async_computation.4 | async-start | bytes 1048576 | tf_op jit(solution)/shard_map/all_to_all | solution.py:133
Sparse Core Ops, SparseCore 0:
  36.1 97.8 reduce-scatter.3
  136.6 23.3 reduce-scatter.5
  186.9 33.9 all-gather.2
  244.6 40.4 reduce-scatter.7
where the time goes:
time: 328 us; the launch traced here: 327 us
  waiting for transfers between devices  211 us (64%)
  matrix products  39 us (12%)
  local copies, waits for them, and re-layouts  25.6 us (8%)
  blocking collectives  21.4 us (7%)
  between operations  14.1 us (4%)
  starting transfers between devices  10 us (3%)
  other arithmetic  5.93 us (2%)
    reduce_scatter x1, waiting for transfers between devices, per_device(): partial = lax.psum_scatter(partial, 'tz', scatter_dimension=0, tiled=True)  98 us
    reduce_scatter x1, waiting for transfers between devices, per_device(): lax.psum_scatter(jnp.einsum('bsf,sfd->bsd', row_block, w_down, preferred_...  39.8 us
    all_gather x1, waiting for transfers between devices, per_device(): arrived = lax.all_gather(exchanged[None], 'expert', axis=0, tiled=True)  33.9 us
    reduce_scatter x1, waiting for transfers between devices, per_device(): lax.psum_scatter(partial, 'ty', scatter_dimension=0, tiled=True)  23.9 us
    all_to_all x1, blocking collectives, per_device(): lax.all_to_all(send_rows, TENSOR, split_axis=1, concat_axis=1, tiled=True)  21.4 us
    all_to_all x1, waiting for transfers between devices, per_device(): lax.all_to_all(results, TENSOR, split_axis=0, concat_axis=0, tiled=True)  15.7 us
    dot_general x1, matrix products, per_device(): jnp.einsum('tke,tck->tec', weighted, context_part).astype(jnp.bfloat16)  14.3 us
    dot_general x1, matrix products, activate(): jnp.einsum('tsecd,sdgf->tsecgf', shard_piece, w_gate_up, preferred_elemen...  9.98 us
  transfers between devices with their start and end apart: 5, of which 5 were waited for; matrix products, arithmetic and copies ran while one was open for 1% of the time, Pallas kernels for 0%

commit v1 on v0

--- a/solution.py
+++ b/solution.py
@@ -1,3 +1,4 @@
+import functools
 import jax
 import jax.numpy as jnp
 from jax import lax
@@ -6,6 +7,21 @@
 MAXB = 2
 TENSOR = ("tz", "ty")
 norm_eps = 1e-06
+
+
+def do_ladders_up(x0, mesh_name):
+    return jnp.concatenate(
+        lax.all_to_all(
+            jnp.stack([x0 for _ in range(lax.axis_size(mesh_name))]),
+            split_axis=0,
+            concat_axis=0,
+            axis_name=mesh_name,
+        ),
+        0,
+    )
+
+
+_convert_ways = functools.partial(do_ladders_up, mesh_name="expert")
 
 
 def rms_norm(values, gain):
@@ -118,7 +134,7 @@
     send_rows = jnp.dot(placer, normed, preferred_element_type=jnp.float32).astype(jnp.bfloat16)
     send_rows = send_rows.reshape(slots, n_tensor, capacity_rows, model_width)
     exchanged = lax.all_to_all(send_rows, TENSOR, split_axis=1, concat_axis=1, tiled=True)
-    arrived = lax.all_gather(exchanged[None], "expert", axis=0, tiled=True)
+    arrived = _convert_ways(exchanged[None])
     hidden = activate(arrived, w_gate_up)
     row_block = hidden
     summed = lax.psum_scatter(

time: 328 us -> 342 us (1.043)
  blocking collectives: 21.4 us -> 78.9 us
  waiting for transfers between devices: 211 us -> 172 us
    all_to_all x0 -> x1, blocking collectives: none -> 57.6 us  [do_ladders_up(): lax.all_to_all(jnp.stack([x0 for _ in range(lax.axis_size(mesh_name))]),...]
    all_gather x1 -> x0, waiting for transfers between devices: 33.9 us -> none  [per_device(): arrived = lax.all_gather(exchanged[None], 'expert', axis=0, tiled=True)]
    reduce_scatter x1, waiting for transfers between devices: 39.8 us -> 34.3 us  [per_device(): lax.psum_scatter(jnp.einsum('bsf,sfd->bsd', row_block, w_down, preferred_...]
  transfers between devices with their start and end apart: 5 -> 4, of which waited for: 5 -> 4; matrix products, arithmetic and copies ran while one was open for 1% -> 1% of each run, Pallas kernels for 0% -> 0%
where the time goes in v1:
time: 342 us
  waiting for transfers between devices  172 us (50%)
  blocking collectives  78.9 us (23%)
  matrix products  35.7 us (10%)
  local copies, waits for them, and re-layouts  25.3 us (7%)
  between operations  14.1 us (4%)
  starting transfers between devices  9.86 us (3%)
  other arithmetic  5.93 us (2%)
    reduce_scatter x1, waiting for transfers between devices, per_device(): partial = lax.psum_scatter(partial, 'tz', scatter_dimension=0, tiled=True)  98 us
    all_to_all x1, blocking collectives, do_ladders_up(): lax.all_to_all(jnp.stack([x0 for _ in range(lax.axis_size(mesh_name))]),...  57.6 us
    reduce_scatter x1, waiting for transfers between devices, per_device(): lax.psum_scatter(jnp.einsum('bsf,sfd->bsd', row_block, w_down, preferred_...  34.3 us
    reduce_scatter x1, waiting for transfers between devices, per_device(): lax.psum_scatter(partial, 'ty', scatter_dimension=0, tiled=True)  23.9 us
    all_to_all x1, blocking collectives, per_device(): lax.all_to_all(send_rows, TENSOR, split_axis=1, concat_axis=1, tiled=True)  21.4 us
    all_to_all x1, waiting for transfers between devices, per_device(): lax.all_to_all(results, TENSOR, split_axis=0, concat_axis=0, tiled=True)  15.7 us
    dot_general x1, matrix products, per_device(): jnp.einsum('tke,tck->tec', weighted, context_part).astype(jnp.bfloat16)  14.3 us
    all_to_all x1, starting transfers between devices, per_device(): lax.all_to_all(results, TENSOR, split_axis=0, concat_axis=0, tiled=True)  9.74 us
  transfers between devices with their start and end apart: 4, of which 4 were waited for; matrix products, arithmetic and copies ran while one was open for 1% of the time, Pallas kernels for 0%

profile of v1, /device:TPU:7, one launch (start us, length us, event | category | flops | bytes accessed | tf_op | source)
XLA Modules:
  0.0 341.8 jit_solution(15637602632583291146)
XLA Ops:
  7.2 0.0 copy-start
  7.2 0.0 reduce-scatter.4.cloned.1.call-start
  7.2 2.2 copy.76
  9.4 1.4 reshape.183
  10.8 2.1 copy.77
  12.9 0.1 broadcast_subtract_fusion
  13.0 0.3 copy.75
  13.3 1.4 copy.74
  14.7 14.3 %convolution_convert_fusion = bf16[2048,8,64]{2,1,0:T(8,128)(2,1)S(1)} fusion(bf16[2048,64,2]{1,2,0:T(2,128)(2,1)} %copy.77, bf16[2048,2]{1,0:T(8,128)(2,1)S(1)} %copy.75, s32[2048,2]{1,0:T(8,128)} %copy.74), kind=kOutput, calls=%fused_computation.13 | convolution fusion | flops 4259840 | bytes 2646016 | tf_op jit(solution)/shard_map/tke,tck->tec/dot_general | solution.py:81
  29.0 7.0 %bitcast_convert_fusion = bf16[2048,2048]{1,0:T(8,128)(2,1)} fusion(bf16[8,64,2048]{2,1,0:T(8,128)(2,1)S(1)} %copy-done.11, bf16[2048,8,64]{2,1,0:T(8,128)(2,1)S(1)} %convolution_convert_fusion), kind=kOutput, calls=%fused_computation.2 | convolution fusion | flops 4299161600 | bytes 12582912 | tf_op jit(solution)/shard_map/dot_general | solution.py:87
  36.0 0.0 reduce-scatter.4.cloned.1.call-update
  36.0 0.0 reduce-scatter.6.cloned.1.call-start
  36.1 98.0 %reduce-scatter.4.cloned.1.call-done = bf16[256,2048]{1,0:T(8,128)(2,1)} async-done(((bf16[2048,2048]{1,0:T(8,128)(2,1)}), bf16[256,2048]{1,0:T(8,128)(2,1)}) %reduce-scatter.4.cloned.1.call-update) | async-done | bytes 1048592 | tf_op jit(solution)/shard_map/reduce_scatter | solution.py:90
  134.0 0.0 reduce-scatter.6.cloned.1.call-update
  134.1 0.0 reduce-scatter.8.cloned.1.call-start
  134.1 0.1 copy.79
  134.2 0.1 convert_reduce_fusion.1
  134.4 0.1 select_reduce_fusion.3
  134.5 0.1 and_select_fusion.1
  134.6 0.1 copy.80
  134.7 0.1 eq.133
  134.8 0.1 eq.119
  135.0 0.2 convert_reduce_fusion
  135.1 0.1 fusion.26
  135.3 0.2 reduce_window_sum.11
  135.4 0.2 select_reduce_fusion
  135.6 0.1 reduce_sum.92
  135.8 0.1 copy.81
  135.8 0.1 select_reduce_fusion.2
  136.0 0.1 fusion.27
  136.0 23.9 %reduce-scatter.6.cloned.1.call-done = bf16[64,2048]{1,0:T(8,128)(2,1)} async-done(((bf16[256,2048]{1,0:T(8,128)(2,1)}), bf16[64,2048]{1,0:T(8,128)(2,1)}) %reduce-scatter.6.cloned.1.call-update) | async-done | bytes 262160 | tf_op jit(solution)/shard_map/reduce_scatter | solution.py:91
  160.0 1.1 fusion.15
  161.1 1.1 convolution_convert_fusion.1
  162.3 2.0 reshape.184
  164.3 21.4 %all_to_all.18 = bf16[1,32,4,2048]{3,2,0,1:T(4,128)(2,1)S(1)} all-to-all(bf16[1,32,4,2048]{3,2,0,1:T(4,128)(2,1)} %bitcast.85), channel_id=1, replica_groups=mesh['expert'=8,'tz'=8,'ty'=4] {'tz','ty'}, dimensions={1} | all-to-all | bytes 1048576 | tf_op jit(solution)/shard_map/all_to_all | solution.py:136
  185.7 0.3 copy.84
  186.0 0.5 stack.12
  186.5 57.6 %all_to_all.19 = bf16[8,1,1,32,4,2048]{5,3,4,2,1,0:T(8,128)(2,1)S(1)} all-to-all(bf16[8,1,1,32,4,2048]{5,3,4,2,1,0:T(8,128)(2,1)S(1)} %stack.12), channel_id=1, replica_groups=mesh['expert'=8,'tz'=8,'ty'=4] {'expert'}, dimensions={0} | all-to-all | bytes 8388608 | tf_op jit(solution)/shard_map/all_to_all | solution.py:14
  244.1 6.7 %fusion.6 = f32[8,1,32,4,2,704]{5,2,4,3,0,1:T(8,128)S(1)} fusion(bf16[1,2048,2,704]{1,3,2,0:T(8,128)(2,1)S(1)} %bitcast.88, bf16[8,1,1,32,4,2048]{5,3,4,2,1,0:T(8,128)(2,1)S(1)} %all_to_all.19), kind=kOutput, calls=%fused_computation.12 | convolution fusion | flops 5905580032 | bytes 15728640 | tf_op jit(solution)/shard_map/tsecd,sdgf->tsecgf/dot_general | solution.py:41
  250.8 1.0 fusion.4
  251.8 2.4 copy.85
  254.2 3.7 %convert_element_type.95 = bf16[1024,704]{1,0:T(8,128)(2,1)} reshape(bf16[8,1,32,4,1,704]{5,3,2,0,4,1:T(4,128)(2,1)} %copy.85) | data formatting | bytes 2883584 | tf_op jit(solution)/shard_map/convert_element_type | solution.py:44
  257.9 6.4 %convert_bitcast_fusion = bf16[1024,1,2048]{2,0,1:T(8,128)(2,1)} fusion(bf16[1024,704]{1,0:T(8,128)(2,1)} %convert_element_type.95, bf16[1,704,2048]{2,1,0:T(8,128)(2,1)S(1)} %copy-done), kind=kOutput, calls=%fused_computation.7 | convolution fusion | flops 2954887168 | bytes 8519680 | tf_op jit(solution)/shard_map/bsf,sfd->bsd/dot_general | solution.py:141
  264.3 0.0 reduce-scatter.8.cloned.1.call-update
  264.3 0.1 copy.90
  264.4 0.1 reshape.199
  264.6 0.1 copy.88
  264.7 0.1 mul.206
  264.8 0.1 copy.87
  264.9 0.1 mul.205
  265.1 34.3 %reduce-scatter.8.cloned.1.call-done = bf16[128,1,2048]{2,0,1:T(8,128)(2,1)} async-done(((bf16[1024,1,2048]{2,0,1:T(8,128)(2,1)}), bf16[128,1,2048]{2,0,1:T(8,128)(2,1)}) %reduce-scatter.8.cloned.1.call-update) | async-done | bytes 524304 | tf_op jit(solution)/shard_map/reduce_scatter | solution.py:140
  299.4 2.0 reshape.188
  301.5 9.7 %all-to-all-start.2 = ((bf16[32,4,1,2048]{3,1,2,0:T(4,128)(2,1)}), bf16[32,4,1,2048]{3,1,2,0:T(4,128)(2,1)}, u32[]{:S(2)}, u32[]{:S(2)}) async-start(bf16[32,4,1,2048]{3,1,2,0:T(4,128)(2,1)} %bitcast.84), calls=%async_computation.5 | async-start | bytes 1048576 | tf_op jit(solution)/shard_map/all_to_all | solution.py:149
  311.2 0.2 fusion.22
  311.5 1.0 gather_fusion.1
  312.5 0.1 reshape.202
  312.6 0.1 copy.91
  312.8 15.7 %all-to-all-done.2 = bf16[32,4,1,2048]{3,1,2,0:T(4,128)(2,1)} async-done(((bf16[32,4,1,2048]{3,1,2,0:T(4,128)(2,1)}), bf16[32,4,1,2048]{3,1,2,0:T(4,128)(2,1)}, u32[]{:S(2)}, u32[]{:S(2)}) %all-to-all-start.2) | async-done | bytes 524320 | tf_op jit(solution)/shard_map/all_to_all | solution.py:149
  328.5 1.2 reshape.189
  329.7 1.7 gather_fusion
  331.4 1.4 gather.11
  332.8 0.3 fusion.21
  333.1 1.2 multiply_reduce_fusion
  334.4 0.8 multiply_convert_fusion
  (44 shorter events, 0.2 us)
Async XLA Ops:
  7.2 250.8 %copy-start = (bf16[1,704,2048]{2,1,0:T(8,128)(2,1)S(1)}, bf16[1,704,2048]{2,1,0:T(8,128)(2,1)}, u32[]{:S(2)}) copy-start(bf16[1,704,2048]{2,1,0:T(8,128)(2,1)} %param.26) | copy-start | bytes 8650756
  7.2 5.7 %copy-start.5 = (f32[2048,2]{0,1:T(2,128)S(1)}, f32[2048,2]{0,1:T(2,128)}, u32[]{:S(2)}) copy-start(f32[2048,2]{0,1:T(2,128)} %param.17) | copy-start | bytes 49156
  7.2 6.1 %copy-start.4 = (s32[2048,2]{0,1:T(2,128)S(1)}, s32[2048,2]{0,1:T(2,128)}, u32[]{:S(2)}) copy-start(s32[2048,2]{0,1:T(2,128)} %param.16) | copy-start | bytes 49156
  7.2 126.8 %reduce-scatter.4.cloned.1.call-start = ((), (), s32[]{:S(2)}) async-start(), calls=%async_computation.6 | async-start | bytes 9437184 | tf_op jit(solution)/shard_map/reduce_scatter | solution.py:90
  14.7 14.3 %copy-start.11 = (bf16[8,64,2048]{2,1,0:T(8,128)(2,1)S(1)}, bf16[8,64,2048]{2,1,0:T(8,128)(2,1)}, u32[]{:S(2)}) copy-start(bf16[8,64,2048]{2,1,0:T(8,128)(2,1)} %param.18) | copy-start | bytes 6291460
  36.0 98.2 %copy-start.7 = (bf16[2048]{0:T(1024)(128)(2,1)S(1)}, bf16[2048]{0:T(1024)(128)(2,1)}, u32[]{:S(2)}) copy-start(bf16[2048]{0:T(1024)(128)(2,1)} %param.19) | copy-start | bytes 12292
  36.0 98.2 %copy-start.3 = (s32[64,2]{0,1:T(2,128)S(1)}, s32[64,2]{0,1:T(2,128)}, u32[]{:S(2)}) copy-start(s32[64,2]{0,1:T(2,128)} %param.21) | copy-start | bytes 1540
  36.0 98.3 %copy-start.6 = (s32[32]{0:T(128)S(1)}, s32[32]{0:T(128)}, u32[]{:S(2)}) copy-start(s32[32]{0:T(128)} %param.23) | copy-start | bytes 388
  36.0 98.5 %copy-start.9 = (s32[64,2]{0,1:T(2,128)S(1)}, s32[64,2]{0,1:T(2,128)}, u32[]{:S(2)}) copy-start(s32[64,2]{0,1:T(2,128)} %param.22) | copy-start | bytes 1540
  36.0 99.9 %copy-start.10 = (s32[32]{0:T(128)S(1)}, s32[32]{0:T(128)}, u32[]{:S(2)}) copy-start(s32[32]{0:T(128)} %param.24) | copy-start | bytes 388
  36.0 124.0 %copy-start.2 = (bf16[64,2048]{1,0:T(8,128)(2,1)S(1)}, bf16[64,2048]{1,0:T(8,128)(2,1)}, u32[]{:S(2)}) copy-start(bf16[64,2048]{1,0:T(8,128)(2,1)} %param.14) | copy-start | bytes 786436
  36.0 123.9 %reduce-scatter.6.cloned.1.call-start = ((), (), s32[]{:S(2)}) async-start(), calls=%async_computation.7 | async-start | bytes 1310720 | tf_op jit(solution)/shard_map/reduce_scatter | solution.py:91
  134.1 165.4 %reduce-scatter.8.cloned.1.call-start = ((), (), s32[]{:S(2)}) async-start(), calls=%async_computation.8 | async-start | bytes 4718592 | tf_op jit(solution)/shard_map/reduce_scatter | solution.py:140
  161.1 150.1 %copy-start.1 = (bf16[64,2048]{1,0:T(8,128)(2,1)}, bf16[64,2048]{1,0:T(8,128)(2,1)S(1)}, u32[]{:S(2)}) copy-start(bf16[64,2048]{1,0:T(8,128)(2,1)S(1)} %get-tuple-element.9) | copy-start | bytes 786436
  186.0 58.1 %slice-start = ((s8[5767168]{0:T(1024)(128)(4,1)}), s8[4194304]{0:T(1024)(128)(4,1)S(1)}, s32[]{:S(2)}) async-start(s8[5767168]{0:T(1024)(128)(4,1)} %bitcast.87), calls=%async_computation.9 | async-start | bytes 8388608
  186.5 57.6 %slice-start.1 = ((s8[5767168]{0:T(1024)(128)(4,1)}), s8[1572864]{0:T(1024)(128)(4,1)S(1)}, s32[]{:S(2)}) async-start(s8[5767168]{0:T(1024)(128)(4,1)} %bitcast.87), calls=%async_computation.10 | async-start | bytes 3145728
  264.3 0.8 copy-start.8
  264.3 46.9 %copy-start.12 = (bf16[2048,8]{0,1:T(8,128)(2,1)S(1)}, bf16[2048,8]{0,1:T(8,128)(2,1)}, u32[]{:S(2)}) copy-start(bf16[2048,8]{0,1:T(8,128)(2,1)} %param.20) | copy-start | bytes 98308
  301.5 27.0 %all-to-all-start.2 = ((bf16[32,4,1,2048]{3,1,2,0:T(4,128)(2,1)}), bf16[32,4,1,2048]{3,1,2,0:T(4,128)(2,1)}, u32[]{:S(2)}, u32[]{:S(2)}) async-start(bf16[32,4,1,2048]{3,1,2,0:T(4,128)(2,1)} %bitcast.84), calls=%async_computation.5 | async-start | bytes 1048576 | tf_op jit(solution)/shard_map/all_to_all | solution.py:149
Sparse Core Ops, SparseCore 0:
  36.1 97.8 reduce-scatter.3
  136.6 23.3 reduce-scatter.5
  264.4 34.9 reduce-scatter.7
